TPU v7x, 256 devices: a whole 4x4x8 slice. The times are simulated.
256 devices in a mesh: gx: 16 (over z, core), gy: 16 (over y, x).
Axes of the slice: x: 4, y: 4, z: 8, core: 2. Of those that a mesh axis runs over, the one named last changes fastest.
Arguments:
- field: float32 [64, 4096, 128], P('gy', 'gx'), may hold values from -5 to 5
- courant: float32 [3, 64, 4096, 128], P(None, 'gy', 'gx'), may hold values from -2.5 to 2.5
- diffusion_number: float32 [64, 4096, 128], P('gy', 'gx'), may hold values from 65536 to 1310720
Outputs:
- solved: float32 [64, 4096, 128], P('gy', 'gx')
All inputs are finite; a program needn't handle non-finite values.
Results may differ from a plain program's by a relative error of at most 0.0013.
Values sent between devices are 32-bit elements; how exact they have to be, the bound alone decides.
No kernel may reach another device: no remote copies, remote signals or barrier semaphores. Data moves between devices by JAX's collectives and lax.ppermute only.
A program may use at most 64 MiB of HBM per device.

v0:
```python
import jax
import jax.numpy as jnp
from jax import lax
from jax.sharding import PartitionSpec as P


def padded_2(cells, sides, width, closed):
    for axis, dim in sides:
        count = lax.axis_size(axis)
        ends = count if closed else count - 1
        head = lax.slice_in_dim(cells, 0, width, axis=dim)
        tail = lax.slice_in_dim(cells, cells.shape[dim] - width, cells.shape[dim], axis=dim)
        cells = jnp.concatenate(
            [
                lax.ppermute(tail, axis, [(i, (i + 1) % count) for i in range(ends)]),
                cells,
                lax.ppermute(head, axis, [((i + 1) % count, i) for i in range(ends)]),
            ],
            axis=dim,
        )
    return cells


def difference_pair(padded, sweep_direction, length):
    shifted = [
        lax.slice_in_dim(padded, offset, offset + length, axis=sweep_direction)
        for offset in range(5)
    ]
    gradient = (8.0 * (shifted[3] - shifted[1]) - (shifted[4] - shifted[0])) / 12.0
    curvature = (
        16.0 * (shifted[3] + shifted[1]) - (shifted[4] + shifted[0]) - 30.0 * shifted[2]
    ) / 12.0
    return (gradient, curvature)


def build_rhs(field, courant, y_padded, x_padded):
    z_padded = jnp.concatenate([field[:, :, -2:], field, field[:, :, :2]], 2)
    grad_y, curve_y = difference_pair(y_padded, 0, field.shape[0])
    grad_x = difference_pair(x_padded, 1, field.shape[1])[0]
    grad_z, curve_z = difference_pair(z_padded, 2, field.shape[2])
    transport = courant[0] * grad_x + courant[1] * grad_y + courant[2] * grad_z
    return field - transport + 0.05 * (curve_y + curve_z) + 0.3 * field / (1.0 + field * field)


def rows_below(values, stride, fill, sweep_direction):
    length = values.shape[sweep_direction]
    filler = jnp.full_like(lax.slice_in_dim(values, 0, stride, axis=sweep_direction), fill)
    return jnp.concatenate(
        [filler, lax.slice_in_dim(values, 0, length - stride, axis=sweep_direction)],
        sweep_direction,
    )


def rows_above(values, stride, fill, sweep_direction):
    length = values.shape[sweep_direction]
    filler = jnp.full_like(
        lax.slice_in_dim(values, length - stride, length, axis=sweep_direction), fill
    )
    return jnp.concatenate(
        [lax.slice_in_dim(values, stride, length, axis=sweep_direction), filler], sweep_direction
    )


def combine_rows(own_rows, below_set, above_set):
    lower_band, main_diagonal, upper_band, right_hand_sides = own_rows
    low_sub, low_diag, low_super, low_rights = below_set
    high_sub, high_diag, high_super, high_rights = above_set
    factor_low = -lower_band / low_diag
    factor_high = -upper_band / high_diag
    new_sub = factor_low * low_sub
    new_super = factor_high * high_super
    new_diag = main_diagonal + factor_low * low_super + factor_high * high_sub
    new_rights = tuple(
        (
            value + factor_low * lower_value + factor_high * upper_value
            for value, lower_value, upper_value in zip(right_hand_sides, low_rights, high_rights)
        )
    )
    return (new_sub, new_diag, new_super, new_rights)


def parallel_cyclic_reduction(
    lower_band, main_diagonal, upper_band, right_hand_sides, sweep_direction
):
    length = main_diagonal.shape[sweep_direction]
    stride = 1
    while stride < length:
        below_set = (
            rows_below(lower_band, stride, 0.0, sweep_direction),
            rows_below(main_diagonal, stride, 1.0, sweep_direction),
            rows_below(upper_band, stride, 0.0, sweep_direction),
            tuple((rows_below(value, stride, 0.0, sweep_direction) for value in right_hand_sides)),
        )
        above_set = (
            rows_above(lower_band, stride, 0.0, sweep_direction),
            rows_above(main_diagonal, stride, 1.0, sweep_direction),
            rows_above(upper_band, stride, 0.0, sweep_direction),
            tuple((rows_above(value, stride, 0.0, sweep_direction) for value in right_hand_sides)),
        )
        lower_band, main_diagonal, upper_band, right_hand_sides = combine_rows(
            (lower_band, main_diagonal, upper_band, right_hand_sides), below_set, above_set
        )
        stride = stride * 2
    return tuple((value / main_diagonal for value in right_hand_sides))


def shards(field, courant, diffusion_number):
    y_padded = padded_2(field, (("gy", 0),), 2, True)
    x_padded = padded_2(field, (("gx", 1),), 2, False)
    rhs = build_rhs(field, courant, y_padded, x_padded)
    place = lax.axis_index("gx")
    device_count = lax.axis_size("gx")
    sub_full = -diffusion_number
    diag_full = 1.0 + 2.0 * diffusion_number
    super_full = -diffusion_number
    edge_zeros = jnp.zeros_like(rhs[:, 0:1])
    inner_zeros = jnp.zeros_like(rhs[:, 3:])
    sub_inner = jnp.concatenate([edge_zeros, sub_full[:, 2:-1]], 1)
    super_inner = jnp.concatenate([super_full[:, 1:-2], edge_zeros], 1)
    diag_inner = diag_full[:, 1:-1]
    first_unit = jnp.concatenate([-sub_full[:, 1:2], inner_zeros], 1)
    last_unit = jnp.concatenate([inner_zeros, -super_full[:, -2:-1]], 1)
    particular_solution, first_row_response, last_row_response = parallel_cyclic_reduction(
        sub_inner, diag_inner, super_inner, (rhs[:, 1:-1], first_unit, last_unit), 1
    )
    low_open = (place > 0).astype(jnp.float32)
    high_open = (place < device_count - 1).astype(jnp.float32)
    sub_first = sub_full[:, 0:1] * low_open
    diag_first = diag_full[:, 0:1] + super_full[:, 0:1] * first_row_response[:, 0:1]
    super_first = super_full[:, 0:1] * last_row_response[:, 0:1]
    right_first = rhs[:, 0:1] - super_full[:, 0:1] * particular_solution[:, 0:1]
    sub_last = sub_full[:, -1:] * first_row_response[:, -1:]
    diag_last = diag_full[:, -1:] + sub_full[:, -1:] * last_row_response[:, -1:]
    super_last = super_full[:, -1:] * high_open
    right_last = rhs[:, -1:] - sub_full[:, -1:] * particular_solution[:, -1:]
    reduced_sub = jnp.concatenate([sub_first, sub_last], 1)
    reduced_diag = jnp.concatenate([diag_first, diag_last], 1)
    reduced_super = jnp.concatenate([super_first, super_last], 1)
    reduced_right = jnp.concatenate([right_first, right_last], 1)
    stacked = jnp.concatenate([reduced_sub, reduced_diag, reduced_super, reduced_right], 1)
    gathered = lax.all_gather(stacked, "gx", axis=1, tiled=True)
    gathered = gathered.reshape(gathered.shape[0], device_count, 4, 2, gathered.shape[-1])
    gathered_lower_band, gathered_diagonal, gathered_upper_band, gathered_rhs = (
        gathered[:, :, k].reshape(gathered.shape[0], 2 * device_count, gathered.shape[-1])
        for k in range(4)
    )
    boundary_rows_gathered = parallel_cyclic_reduction(
        gathered_lower_band, gathered_diagonal, gathered_upper_band, (gathered_rhs,), 1
    )[0]
    ends = lax.dynamic_slice_in_dim(boundary_rows_gathered, 2 * place, 2, 1)
    interior = (
        particular_solution + first_row_response * ends[:, 0:1] + last_row_response * ends[:, 1:2]
    )
    return jnp.concatenate([ends[:, 0:1], interior, ends[:, 1:2]], 1)


def solution(mesh):
    in_specs = (P("gy", "gx", None), P(None, "gy", "gx", None), P("gy", "gx", None))
    out_specs = P("gy", "gx", None)
    return jax.shard_map(shards, mesh=mesh, in_specs=in_specs, out_specs=out_specs, check_vma=False)
```

profile of v0, /device:TPU:1, one launch (start us, length us, event | category | flops | bytes accessed | tf_op | source)
XLA Modules:
  0.0 54.8 jit_solution(11624598500980363579)
XLA Ops:
  0.0 1.9 %fusion.76 = (f32[2,256,128]{2,1,0:T(8,128)}, f32[2,256,128]{2,1,0:T(8,128)}) fusion(f32[4,256,128]{2,1,0:T(8,128)} %param.3), kind=kLoop, calls=%fused_computation.204 | loop fusion | bytes 1048576 | tf_op jit(solution)/shard_map/slice | solution.py:11
  1.9 2.0 %collective-permute-start.3 = (f32[2,256,128]{2,1,0:T(8,128)}, f32[2,256,128]{2,1,0:T(8,128)}, u32[]{:S(2)}, u32[]{:S(2)}) collective-permute-start(f32[2,256,128]{2,1,0:T(8,128)} %get-tuple-element.169), channel_id=1, source_target_pairs={{0,1},{1,2},{2,3},{3,4},{4,5},{5,6},{6,7},{7,8},{8,9},{9,10},{10,1... | collective-permute-start | bytes 786440 | tf_op jit(solution)/shard_map/ppermute | solution.py:15
  3.9 3.7 %collective-permute-start.2 = (f32[2,256,128]{2,1,0:T(8,128)}, f32[2,256,128]{2,1,0:T(8,128)S(1)}, u32[]{:S(2)}, u32[]{:S(2)}) collective-permute-start(f32[2,256,128]{2,1,0:T(8,128)} %get-tuple-element.168), channel_id=1, source_target_pairs={{1,0},{2,1},{3,2},{4,3},{5,4},{6,5},{7,6},{8,7},{9,8},{10,9},{11,1... | collective-permute-start | bytes 786440 | tf_op jit(solution)/shard_map/ppermute | solution.py:17
  7.6 0.7 %fusion.78 = (f32[4,2,128]{2,1,0:T(2,128)S(1)}, f32[4,2,128]{2,1,0:T(2,128)S(1)}) fusion(f32[4,256,128]{2,1,0:T(8,128)} %param.3), kind=kLoop, calls=%fused_computation.206 | loop fusion | bytes 16384 | tf_op jit(solution)/shard_map/slice | solution.py:11
  8.4 4.7 %collective-permute-start = (f32[4,2,128]{2,1,0:T(2,128)S(1)}, f32[4,2,128]{2,1,0:T(2,128)S(1)}, u32[]{:S(2)}, u32[]{:S(2)}) collective-permute-start(f32[4,2,128]{2,1,0:T(2,128)S(1)} %get-tuple-element.175), channel_id=1, source_target_pairs={{16,0},{32,16},{48,32},{64,48},{80,64},{96,80},{112,96},{128,112},... | collective-permute-start | bytes 12296 | tf_op jit(solution)/shard_map/ppermute | solution.py:17
  13.1 1.9 %collective-permute-start.1 = (f32[4,2,128]{2,1,0:T(2,128)S(1)}, f32[4,2,128]{2,1,0:T(2,128)S(1)}, u32[]{:S(2)}, u32[]{:S(2)}) collective-permute-start(f32[4,2,128]{2,1,0:T(2,128)S(1)} %get-tuple-element.176), channel_id=1, source_target_pairs={{0,16},{16,32},{32,48},{48,64},{64,80},{80,96},{96,112},{112,128},... | collective-permute-start | bytes 12296 | tf_op jit(solution)/shard_map/ppermute | solution.py:15
  15.0 1.1 %multiply_add_fusion.26 = (f32[4,256,128]{2,1,0:T(8,128)S(1)}, f32[4,256,128]{2,1,0:T(8,128)S(1)}) fusion(f32[4,256,128]{2,1,0:T(8,128)} %param.5), kind=kLoop, calls=%fused_computation.95 | loop fusion | flops 393216 | bytes 1572864 | tf_op jit(solution)/shard_map/add | solution.py:114
  16.1 1.2 %fusion.73 = (f32[4,253,128]{2,1,0:T(8,128)S(1)}, f32[4,253,128]{2,1,0:T(8,128)S(1)}, f32[4,253,128]{2,1,0:T(8,128)}, f32[4,253,128]{2,1,0:T(8,128)}) fusion(f32[4,256,128]{2,1,0:T(8,128)S(1)} %get-tuple-element.165, f32[4,256,128]{2,1,0:T(8,128)S(1)} %get-tuple-element.164), kind=kLoop, calls=%fused_computation.201 | loop fusion | bytes 4145152 | tf_op jit(solution)/shard_map/slice | solution.py:119
  17.4 0.8 %pad_slice_fusion.9 = f32[4,253,128]{2,1,0:T(8,128)} fusion(f32[4,253,128]{2,1,0:T(8,128)S(1)} %get-tuple-element.161), kind=kLoop, calls=%fused_computation.97 | loop fusion | bytes 1036288 | tf_op jit(solution)/shard_map/slice | solution.py:49
  18.3 1.1 %pad_slice_fusion.4 = (f32[4,253,128]{2,1,0:T(8,128)}, f32[4,253,128]{2,1,0:T(8,128)}) fusion(f32[4,1,128]{2,1,0:T(1,128)S(1)} %get-tuple-element.93, f32[4,1,128]{2,1,0:T(1,128)S(1)} %get-tuple-element.94), kind=kLoop, calls=%fused_computation.4 | loop fusion | bytes 1040384 | tf_op jit(solution)/shard_map/slice | solution.py:60
  19.5 1.1 %constant_dynamic-update-slice_fusion.5 = f32[6,256,128]{2,1,0:T(8,128)S(1)} fusion(f32[2,256,128]{2,1,0:T(8,128)} %collective-permute-done.3), kind=kLoop, calls=%fused_computation.133 | loop fusion | bytes 524288
  21.0 1.2 %fusion.10 = f32[4,256,128]{2,1,0:T(8,128)S(1)} fusion(f32[4,256,128]{2,1,0:T(8,128)S(1)} %copy-done, f32[4,2,128]{2,1,0:T(2,128)S(1)} %collective-permute-done.1, f32[4,258,128]{2,1,0:T(8,128)S(1)} %constant_dynamic-update-slice_fusion, f32[4,256,2]{2,1,0:T(8,128)S(1)} %get-tuple-element.174, f32[4,256,2]{2,1,0:T(8,128)S(1)} %get-tuple-element.173, ...), kind=kLoop, calls=%fused_computation.20 | loop fusion | flops 6029312 | bytes 5787648 | tf_op jit(solution)/shard_map/add | solution.py:42
  22.3 0.9 %copy-done.4 = f32[4,253,128]{2,1,0:T(8,128)S(1)} copy-done((f32[4,253,128]{2,1,0:T(8,128)S(1)}, f32[4,253,128]{2,1,0:T(8,128)}, u32[]{:S(2)}) %copy-start.4) | copy-done | bytes 518168
  24.1 0.9 %copy-done.1 = f32[4,253,128]{2,1,0:T(8,128)S(1)} copy-done((f32[4,253,128]{2,1,0:T(8,128)S(1)}, f32[4,253,128]{2,1,0:T(8,128)}, u32[]{:S(2)}) %copy-start.1) | copy-done | bytes 518168
  25.3 0.6 %multiply_add_fusion.6 = (f32[4,254,128]{2,1,0:T(8,128)S(1)}, f32[4,254,128]{2,1,0:T(8,128)S(1)}, f32[4,254,128]{2,1,0:T(8,128)S(1)}, f32[4,254,128]{2,1,0:T(8,1...) fusion(f32[4,252,128]{2,1,0:T(8,128)S(1)} %get-tuple-element.159, ...), kind=kLoop, calls=%fused_computation.43 | loop fusion | flops 2340864 | bytes 9343992 | tf_op jit(solution)/shard_map/add | solution.py:75
  26.5 0.9 %multiply_add_fusion.5 = (f32[4,254,128]{2,1,0:T(8,128)S(1)}, f32[4,254,128]{2,1,0:T(8,128)S(1)}, f32[4,254,128]{2,1,0:T(8,128)S(1)}, f32[4,254,128]{2,1,0:T(8,1...) fusion(f32[4,250,128]{2,1,0:T(8,128)S(1)} %get-tuple-element.155, ...), kind=kLoop, calls=%fused_computation.42 | loop fusion | flops 2340864 | bytes 11386880 | tf_op jit(solution)/shard_map/add | solution.py:75
  28.0 0.7 %multiply_add_fusion.4 = (f32[4,254,128]{2,1,0:T(8,128)S(1)}, f32[4,254,128]{2,1,0:T(8,128)S(1)}, f32[4,254,128]{2,1,0:T(8,128)S(1)}, f32[4,254,128]{2,1,0:T(8,1...) fusion(f32[4,246,128]{2,1,0:T(8,128)S(1)} %get-tuple-element.147, ...), kind=kLoop, calls=%fused_computation.41 | loop fusion | flops 2340864 | bytes 11329536 | tf_op jit(solution)/shard_map/add | solution.py:75
  29.3 0.4 multiply_add_fusion.3
  30.3 0.5 multiply_add_fusion.2
  31.4 0.5 multiply_add_fusion.1
  32.2 0.4 multiply_add_fusion.7
  33.1 0.4 add_divide_fusion
  33.6 19.3 %all_gather.3 = f32[4,128,128]{2,1,0:T(8,128)S(1)} all-gather(f32[4,8,128]{2,1,0:T(8,128)S(1)} %concatenate.548), channel_id=1, replica_groups=mesh['gx'=16,'gy'=16] {'gx'}, dimensions={1}, use_global_device_ids=true | all-gather | bytes 278528 | tf_op jit(solution)/shard_map/all_gather | solution.py:141
  54.0 0.8 %pad_maximum_fusion.3 = f32[4,256,128]{2,1,0:T(8,128)} fusion(f32[4,1,128]{2,1,0:T(1,128)S(1)} %get-tuple-element.223, f32[4,254,128]{2,1,0:T(8,128)S(1)} %multiply_add_fusion, f32[4,1,128]{2,1,0:T(1,128)S(1)} %get-tuple-element.222), kind=kLoop, calls=%fused_computation.33 | loop fusion | flops 262144 | bytes 1048576 | tf_op jit(solution)/shard_map/concatenate | solution.py:154
  (108 shorter events, 6.2 us)
Async XLA Ops:
  1.9 17.7 %collective-permute-start.3 = (f32[2,256,128]{2,1,0:T(8,128)}, f32[2,256,128]{2,1,0:T(8,128)}, u32[]{:S(2)}, u32[]{:S(2)}) collective-permute-start(f32[2,256,128]{2,1,0:T(8,128)} %get-tuple-element.169), channel_id=1, source_target_pairs={{0,1},{1,2},{2,3},{3,4},{4,5},{5,6},{6,7},{7,8},{8,9},{9,10},{10,1... | collective-permute-start | bytes 786440 | tf_op jit(solution)/shard_map/ppermute | solution.py:15
  3.9 16.8 %collective-permute-start.2 = (f32[2,256,128]{2,1,0:T(8,128)}, f32[2,256,128]{2,1,0:T(8,128)S(1)}, u32[]{:S(2)}, u32[]{:S(2)}) collective-permute-start(f32[2,256,128]{2,1,0:T(8,128)} %get-tuple-element.168), channel_id=1, source_target_pairs={{1,0},{2,1},{3,2},{4,3},{5,4},{6,5},{7,6},{8,7},{9,8},{10,9},{11,1... | collective-permute-start | bytes 786440 | tf_op jit(solution)/shard_map/ppermute | solution.py:17
  8.4 12.4 %collective-permute-start = (f32[4,2,128]{2,1,0:T(2,128)S(1)}, f32[4,2,128]{2,1,0:T(2,128)S(1)}, u32[]{:S(2)}, u32[]{:S(2)}) collective-permute-start(f32[4,2,128]{2,1,0:T(2,128)S(1)} %get-tuple-element.175), channel_id=1, source_target_pairs={{16,0},{32,16},{48,32},{64,48},{80,64},{96,80},{112,96},{128,112},... | collective-permute-start | bytes 12296 | tf_op jit(solution)/shard_map/ppermute | solution.py:17
  13.1 7.7 %collective-permute-start.1 = (f32[4,2,128]{2,1,0:T(2,128)S(1)}, f32[4,2,128]{2,1,0:T(2,128)S(1)}, u32[]{:S(2)}, u32[]{:S(2)}) collective-permute-start(f32[4,2,128]{2,1,0:T(2,128)S(1)} %get-tuple-element.176), channel_id=1, source_target_pairs={{0,16},{16,32},{32,48},{48,64},{64,80},{80,96},{96,112},{112,128},... | collective-permute-start | bytes 12296 | tf_op jit(solution)/shard_map/ppermute | solution.py:15
  17.4 2.0 %copy-start = (f32[4,256,128]{2,1,0:T(8,128)S(1)}, f32[4,256,128]{2,1,0:T(8,128)}, u32[]{:S(2)}) copy-start(f32[4,256,128]{2,1,0:T(8,128)} %param.3) | copy-start | bytes 1572868
  19.5 1.5 %copy-start.6 = (f32[3,4,256,128]{3,2,1,0:T(8,128)S(1)}, f32[3,4,256,128]{3,2,1,0:T(8,128)}, u32[]{:S(2)}) copy-start(f32[3,4,256,128]{3,2,1,0:T(8,128)} %param.4) | copy-start | bytes 4718596
  22.2 1.0 %copy-start.4 = (f32[4,253,128]{2,1,0:T(8,128)S(1)}, f32[4,253,128]{2,1,0:T(8,128)}, u32[]{:S(2)}) copy-start(f32[4,253,128]{2,1,0:T(8,128)} %get-tuple-element.224) | copy-start | bytes 1554436
  22.2 1.2 %copy-start.5 = (f32[4,253,128]{2,1,0:T(8,128)S(1)}, f32[4,253,128]{2,1,0:T(8,128)}, u32[]{:S(2)}) copy-start(f32[4,253,128]{2,1,0:T(8,128)} %get-tuple-element.225) | copy-start | bytes 1554436
  24.0 1.0 %copy-start.1 = (f32[4,253,128]{2,1,0:T(8,128)S(1)}, f32[4,253,128]{2,1,0:T(8,128)}, u32[]{:S(2)}) copy-start(f32[4,253,128]{2,1,0:T(8,128)} %pad_slice_fusion.9) | copy-start | bytes 1554436
  24.0 1.2 %copy-start.2 = (f32[4,253,128]{2,1,0:T(8,128)S(1)}, f32[4,253,128]{2,1,0:T(8,128)}, u32[]{:S(2)}) copy-start(f32[4,253,128]{2,1,0:T(8,128)} %get-tuple-element.226) | copy-start | bytes 1554436
  24.0 1.3 %copy-start.3 = (f32[4,253,128]{2,1,0:T(8,128)S(1)}, f32[4,253,128]{2,1,0:T(8,128)}, u32[]{:S(2)}) copy-start(f32[4,253,128]{2,1,0:T(8,128)} %get-tuple-element.227) | copy-start | bytes 1554436
where the time goes:
time: 55.1 us; the launch traced here: 54.8 us
  blocking collectives  19.3 us (35%)
  local copies, waits for them, and re-layouts  12.8 us (23%)
  starting transfers between devices  12.4 us (23%)
  other arithmetic  9.54 us (17%)
  between operations  0.83 us (2%)
    all_gather x1, blocking collectives, shards(): gathered = lax.all_gather(stacked, 'gx', axis=1, tiled=True)  19.3 us
    ppermute x2, starting transfers between devices, padded_2(): lax.ppermute(head, axis, [((i + 1) % count, i) for i in range(ends)])  8.41 us
    add x11, other arithmetic, combine_rows(): value + factor_low * lower_value + factor_high * upper_value  4.48 us
    ppermute x2, starting transfers between devices, padded_2(): lax.ppermute(tail, axis, [(i, (i + 1) % count) for i in range(ends)])  3.95 us
    unnamed x16, local copies, waits for them, and re-layouts  3.76 us
    slice x40, local copies, waits for them, and re-layouts, rows_below(): lax.slice_in_dim(values, 0, length - stride, axis=sweep_direction)  2.66 us
    slice x2, local copies, waits for them, and re-layouts, padded_2(): head = lax.slice_in_dim(cells, 0, width, axis=dim)  2.62 us
    slice x26, local copies, waits for them, and re-layouts, rows_above(): lax.slice_in_dim(values, stride, length, axis=sweep_direction)  2.09 us
  transfers between devices with their start and end apart: 4, of which 0 were waited for; matrix products, arithmetic and copies ran while one was open for 12% of the time, Pallas kernels for 0%

commit v1 on v0

--- a/solution.py
+++ b/solution.py
@@ -105,6 +105,13 @@
 
 
 def shards(field, courant, diffusion_number):
+
+    def _post_stacks_all(m, row_dim):
+        item_now = jnp.stack([m for _ in range(lax.psum(1, "gx"))], 0)
+        r_now = lax.all_to_all(item_now, "gx", 0, 0)
+        outer = jnp.concatenate(r_now, row_dim)
+        return outer
+
     y_padded = padded_2(field, (("gy", 0),), 2, True)
     x_padded = padded_2(field, (("gx", 1),), 2, False)
     rhs = build_rhs(field, courant, y_padded, x_padded)
@@ -138,7 +145,7 @@
     reduced_super = jnp.concatenate([super_first, super_last], 1)
     reduced_right = jnp.concatenate([right_first, right_last], 1)
     stacked = jnp.concatenate([reduced_sub, reduced_diag, reduced_super, reduced_right], 1)
-    gathered = lax.all_gather(stacked, "gx", axis=1, tiled=True)
+    gathered = _post_stacks_all(stacked, 1)
     gathered = gathered.reshape(gathered.shape[0], device_count, 4, 2, gathered.shape[-1])
     gathered_lower_band, gathered_diagonal, gathered_upper_band, gathered_rhs = (
         gathered[:, :, k].reshape(gathered.shape[0], 2 * device_count, gathered.shape[-1])

time: 55.1 us -> 55 us (level)
  blocking collectives: 19.3 us -> 0 us
  waiting for transfers between devices: 0.01 us -> 11.6 us
  starting transfers between devices: 12.4 us -> 19.9 us
    all_gather x1 -> x0, blocking collectives: 19.3 us -> none  [shards(): gathered = lax.all_gather(stacked, 'gx', axis=1, tiled=True)]
    all_to_all x0 -> x1, waiting for transfers between devices: none -> 11.6 us  [_post_stacks_all(): r_now = lax.all_to_all(item_now, 'gx', 0, 0)]
    all_to_all x0 -> x1, starting transfers between devices: none -> 7.53 us  [_post_stacks_all(): r_now = lax.all_to_all(item_now, 'gx', 0, 0)]
    slice x26, local copies, waits for them, and re-layouts: 2.09 us -> 1.1 us  [rows_above(): lax.slice_in_dim(values, stride, length, axis=sweep_direction)]
    another operation x0 -> x1, local copies, waits for them, and re-layouts: none -> 0.73 us  [_post_stacks_all(): item_now = jnp.stack([m for _ in range(lax.psum(1, 'gx'))], 0)]
    unnamed x16 -> x12, local copies, waits for them, and re-layouts: 3.76 us -> 3.65 us
  transfers between devices with their start and end apart: 4 -> 5, of which waited for: 0 -> 1; matrix products, arithmetic and copies ran while one was open for 12% -> 10% of each run, Pallas kernels for 0% -> 0%
where the time goes in v1:
time: 55 us; the launch traced here: 54.5 us
  starting transfers between devices  19.9 us (36%)
  local copies, waits for them, and re-layouts  12.6 us (23%)
  waiting for transfers between devices  11.6 us (21%)
  other arithmetic  9.56 us (17%)
  between operations  0.84 us (2%)
    all_to_all x1, waiting for transfers between devices, _post_stacks_all(): r_now = lax.all_to_all(item_now, 'gx', 0, 0)  11.6 us
    ppermute x2, starting transfers between devices, padded_2(): lax.ppermute(head, axis, [((i + 1) % count, i) for i in range(ends)])  8.41 us
    all_to_all x1, starting transfers between devices, _post_stacks_all(): r_now = lax.all_to_all(item_now, 'gx', 0, 0)  7.53 us
    add x11, other arithmetic, combine_rows(): value + factor_low * lower_value + factor_high * upper_value  4.5 us
    ppermute x2, starting transfers between devices, padded_2(): lax.ppermute(tail, axis, [(i, (i + 1) % count) for i in range(ends)])  3.95 us
    unnamed x12, local copies, waits for them, and re-layouts  3.65 us
    slice x40, local copies, waits for them, and re-layouts, rows_below(): lax.slice_in_dim(values, 0, length - stride, axis=sweep_direction)  2.66 us
    slice x2, local copies, waits for them, and re-layouts, padded_2(): head = lax.slice_in_dim(cells, 0, width, axis=dim)  2.62 us
  transfers between devices with their start and end apart: 5, of which 1 were waited for; matrix products, arithmetic and copies ran while one was open for 10% of the time, Pallas kernels for 0%

profile of v1, /device:TPU:1, one launch (start us, length us, event | category | flops | bytes accessed | tf_op | source)
XLA Modules:
  0.0 54.5 jit_solution(15803460261263326386)
XLA Ops:
  0.0 1.9 %fusion.76 = (f32[2,256,128]{2,1,0:T(8,128)}, f32[2,256,128]{2,1,0:T(8,128)}) fusion(f32[4,256,128]{2,1,0:T(8,128)} %param.3), kind=kLoop, calls=%fused_computation.204 | loop fusion | bytes 1048576 | tf_op jit(solution)/shard_map/slice | solution.py:11
  1.9 2.0 %collective-permute-start.3 = (f32[2,256,128]{2,1,0:T(8,128)}, f32[2,256,128]{2,1,0:T(8,128)}, u32[]{:S(2)}, u32[]{:S(2)}) collective-permute-start(f32[2,256,128]{2,1,0:T(8,128)} %get-tuple-element.169), channel_id=1, source_target_pairs={{0,1},{1,2},{2,3},{3,4},{4,5},{5,6},{6,7},{7,8},{8,9},{9,10},{10,1... | collective-permute-start | bytes 786440 | tf_op jit(solution)/shard_map/ppermute | solution.py:15
  3.9 3.7 %collective-permute-start.2 = (f32[2,256,128]{2,1,0:T(8,128)}, f32[2,256,128]{2,1,0:T(8,128)S(1)}, u32[]{:S(2)}, u32[]{:S(2)}) collective-permute-start(f32[2,256,128]{2,1,0:T(8,128)} %get-tuple-element.168), channel_id=1, source_target_pairs={{1,0},{2,1},{3,2},{4,3},{5,4},{6,5},{7,6},{8,7},{9,8},{10,9},{11,1... | collective-permute-start | bytes 786440 | tf_op jit(solution)/shard_map/ppermute | solution.py:17
  7.6 0.7 %fusion.78 = (f32[4,2,128]{2,1,0:T(2,128)S(1)}, f32[4,2,128]{2,1,0:T(2,128)S(1)}) fusion(f32[4,256,128]{2,1,0:T(8,128)} %param.3), kind=kLoop, calls=%fused_computation.206 | loop fusion | bytes 16384 | tf_op jit(solution)/shard_map/slice | solution.py:11
  8.4 4.7 %collective-permute-start = (f32[4,2,128]{2,1,0:T(2,128)S(1)}, f32[4,2,128]{2,1,0:T(2,128)S(1)}, u32[]{:S(2)}, u32[]{:S(2)}) collective-permute-start(f32[4,2,128]{2,1,0:T(2,128)S(1)} %get-tuple-element.175), channel_id=1, source_target_pairs={{16,0},{32,16},{48,32},{64,48},{80,64},{96,80},{112,96},{128,112},... | collective-permute-start | bytes 12296 | tf_op jit(solution)/shard_map/ppermute | solution.py:17
  13.1 1.9 %collective-permute-start.1 = (f32[4,2,128]{2,1,0:T(2,128)S(1)}, f32[4,2,128]{2,1,0:T(2,128)S(1)}, u32[]{:S(2)}, u32[]{:S(2)}) collective-permute-start(f32[4,2,128]{2,1,0:T(2,128)S(1)} %get-tuple-element.176), channel_id=1, source_target_pairs={{0,16},{16,32},{32,48},{48,64},{64,80},{80,96},{96,112},{112,128},... | collective-permute-start | bytes 12296 | tf_op jit(solution)/shard_map/ppermute | solution.py:15
  15.0 1.1 %multiply_add_fusion.26 = (f32[4,256,128]{2,1,0:T(8,128)S(1)}, f32[4,256,128]{2,1,0:T(8,128)S(1)}) fusion(f32[4,256,128]{2,1,0:T(8,128)} %param.5), kind=kLoop, calls=%fused_computation.95 | loop fusion | flops 393216 | bytes 1572864 | tf_op jit(solution)/shard_map/add | solution.py:121
  16.1 1.2 %fusion.73 = (f32[4,253,128]{2,1,0:T(8,128)S(1)}, f32[4,253,128]{2,1,0:T(8,128)S(1)}, f32[4,253,128]{2,1,0:T(8,128)}, f32[4,253,128]{2,1,0:T(8,128)}) fusion(f32[4,256,128]{2,1,0:T(8,128)S(1)} %get-tuple-element.165, f32[4,256,128]{2,1,0:T(8,128)S(1)} %get-tuple-element.164), kind=kLoop, calls=%fused_computation.201 | loop fusion | bytes 4145152 | tf_op jit(solution)/shard_map/slice | solution.py:126
  17.4 0.8 %pad_slice_fusion.9 = f32[4,253,128]{2,1,0:T(8,128)} fusion(f32[4,253,128]{2,1,0:T(8,128)S(1)} %get-tuple-element.161), kind=kLoop, calls=%fused_computation.97 | loop fusion | bytes 1036288 | tf_op jit(solution)/shard_map/slice | solution.py:49
  18.7 1.1 %constant_dynamic-update-slice_fusion.5 = f32[6,256,128]{2,1,0:T(8,128)S(1)} fusion(f32[2,256,128]{2,1,0:T(8,128)} %collective-permute-done.3), kind=kLoop, calls=%fused_computation.133 | loop fusion | bytes 524288
  20.2 1.2 %fusion.10 = f32[4,256,128]{2,1,0:T(8,128)S(1)} fusion(f32[4,256,128]{2,1,0:T(8,128)S(1)} %copy-done, f32[4,2,128]{2,1,0:T(2,128)S(1)} %collective-permute-done.1, f32[4,258,128]{2,1,0:T(8,128)S(1)} %constant_dynamic-update-slice_fusion, f32[4,256,2]{2,1,0:T(8,128)S(1)} %get-tuple-element.174, f32[4,256,2]{2,1,0:T(8,128)S(1)} %get-tuple-element.173, ...), kind=kLoop, calls=%fused_computation.20 | loop fusion | flops 6029312 | bytes 5787648 | tf_op jit(solution)/shard_map/add | solution.py:42
  21.5 0.9 %copy-done.2 = f32[4,253,128]{2,1,0:T(8,128)S(1)} copy-done((f32[4,253,128]{2,1,0:T(8,128)S(1)}, f32[4,253,128]{2,1,0:T(8,128)}, u32[]{:S(2)}) %copy-start.2) | copy-done | bytes 518168
  23.3 1.0 %copy-done.1 = f32[4,253,128]{2,1,0:T(8,128)S(1)} copy-done((f32[4,253,128]{2,1,0:T(8,128)S(1)}, f32[4,253,128]{2,1,0:T(8,128)}, u32[]{:S(2)}) %copy-start.1) | copy-done | bytes 518168
  24.2 0.6 %multiply_add_fusion.6 = (f32[4,254,128]{2,1,0:T(8,128)S(1)}, f32[4,254,128]{2,1,0:T(8,128)S(1)}, f32[4,254,128]{2,1,0:T(8,128)S(1)}, f32[4,254,128]{2,1,0:T(8,1...) fusion(f32[4,252,128]{2,1,0:T(8,128)S(1)} %get-tuple-element.159, ...), kind=kLoop, calls=%fused_computation.43 | loop fusion | flops 2340864 | bytes 9343992 | tf_op jit(solution)/shard_map/add | solution.py:75
  25.4 0.9 %multiply_add_fusion.5 = (f32[4,254,128]{2,1,0:T(8,128)S(1)}, f32[4,254,128]{2,1,0:T(8,128)S(1)}, f32[4,254,128]{2,1,0:T(8,128)S(1)}, f32[4,254,128]{2,1,0:T(8,1...) fusion(f32[4,250,128]{2,1,0:T(8,128)S(1)} %get-tuple-element.155, ...), kind=kLoop, calls=%fused_computation.42 | loop fusion | flops 2340864 | bytes 11386880 | tf_op jit(solution)/shard_map/add | solution.py:75
  26.9 0.7 %multiply_add_fusion.4 = (f32[4,254,128]{2,1,0:T(8,128)S(1)}, f32[4,254,128]{2,1,0:T(8,128)S(1)}, f32[4,254,128]{2,1,0:T(8,128)S(1)}, f32[4,254,128]{2,1,0:T(8,1...) fusion(f32[4,246,128]{2,1,0:T(8,128)S(1)} %get-tuple-element.147, ...), kind=kLoop, calls=%fused_computation.41 | loop fusion | flops 2340864 | bytes 11329536 | tf_op jit(solution)/shard_map/add | solution.py:75
  28.2 0.4 multiply_add_fusion.3
  29.2 0.5 multiply_add_fusion.2
  30.3 0.5 multiply_add_fusion.1
  31.0 0.4 multiply_add_fusion.7
  32.5 0.7 %stack.2 = f32[16,4,8,128]{3,2,1,0:T(8,128)} broadcast(f32[4,8,128]{2,1,0:T(8,128)S(1)} %concatenate.548), dimensions={1,2,3} | broadcast | bytes 278528 | tf_op jit(solution)/shard_map/stack | solution.py:110
  33.2 7.5 %all-to-all-start = ((f32[16,4,8,128]{3,2,1,0:T(8,128)}), f32[16,4,8,128]{3,2,1,0:T(8,128)S(1)}, u32[]{:S(2)}, u32[]{:S(2)}) async-start(f32[16,4,8,128]{3,2,1,0:T(8,128)} %stack.2), calls=%async_computation | async-start | bytes 524288 | tf_op jit(solution)/shard_map/all_to_all | solution.py:111
  40.7 11.6 %all-to-all-done = f32[16,4,8,128]{3,2,1,0:T(8,128)S(1)} async-done(((f32[16,4,8,128]{3,2,1,0:T(8,128)}), f32[16,4,8,128]{3,2,1,0:T(8,128)S(1)}, u32[]{:S(2)}, u32[]{:S(2)}) %all-to-all-start) | async-done | bytes 262176 | tf_op jit(solution)/shard_map/all_to_all | solution.py:111
  53.6 0.8 %pad_maximum_fusion.3 = f32[4,256,128]{2,1,0:T(8,128)} fusion(f32[4,1,128]{2,1,0:T(1,128)S(1)} %get-tuple-element.223, f32[4,254,128]{2,1,0:T(8,128)S(1)} %multiply_add_fusion, f32[4,1,128]{2,1,0:T(1,128)S(1)} %get-tuple-element.222), kind=kLoop, calls=%fused_computation.33 | loop fusion | flops 262144 | bytes 1048576 | tf_op jit(solution)/shard_map/concatenate | solution.py:161
  (111 shorter events, 6.7 us)
Async XLA Ops:
  1.9 16.9 %collective-permute-start.3 = (f32[2,256,128]{2,1,0:T(8,128)}, f32[2,256,128]{2,1,0:T(8,128)}, u32[]{:S(2)}, u32[]{:S(2)}) collective-permute-start(f32[2,256,128]{2,1,0:T(8,128)} %get-tuple-element.169), channel_id=1, source_target_pairs={{0,1},{1,2},{2,3},{3,4},{4,5},{5,6},{6,7},{7,8},{8,9},{9,10},{10,1... | collective-permute-start | bytes 786440 | tf_op jit(solution)/shard_map/ppermute | solution.py:15
  3.9 16.0 %collective-permute-start.2 = (f32[2,256,128]{2,1,0:T(8,128)}, f32[2,256,128]{2,1,0:T(8,128)S(1)}, u32[]{:S(2)}, u32[]{:S(2)}) collective-permute-start(f32[2,256,128]{2,1,0:T(8,128)} %get-tuple-element.168), channel_id=1, source_target_pairs={{1,0},{2,1},{3,2},{4,3},{5,4},{6,5},{7,6},{8,7},{9,8},{10,9},{11,1... | collective-permute-start | bytes 786440 | tf_op jit(solution)/shard_map/ppermute | solution.py:17
  8.4 11.6 %collective-permute-start = (f32[4,2,128]{2,1,0:T(2,128)S(1)}, f32[4,2,128]{2,1,0:T(2,128)S(1)}, u32[]{:S(2)}, u32[]{:S(2)}) collective-permute-start(f32[4,2,128]{2,1,0:T(2,128)S(1)} %get-tuple-element.175), channel_id=1, source_target_pairs={{16,0},{32,16},{48,32},{64,48},{80,64},{96,80},{112,96},{128,112},... | collective-permute-start | bytes 12296 | tf_op jit(solution)/shard_map/ppermute | solution.py:17
  13.1 6.9 %collective-permute-start.1 = (f32[4,2,128]{2,1,0:T(2,128)S(1)}, f32[4,2,128]{2,1,0:T(2,128)S(1)}, u32[]{:S(2)}, u32[]{:S(2)}) collective-permute-start(f32[4,2,128]{2,1,0:T(2,128)S(1)} %get-tuple-element.176), channel_id=1, source_target_pairs={{0,16},{16,32},{32,48},{48,64},{64,80},{80,96},{96,112},{112,128},... | collective-permute-start | bytes 12296 | tf_op jit(solution)/shard_map/ppermute | solution.py:15
  17.4 1.2 %copy-start = (f32[4,256,128]{2,1,0:T(8,128)S(1)}, f32[4,256,128]{2,1,0:T(8,128)}, u32[]{:S(2)}) copy-start(f32[4,256,128]{2,1,0:T(8,128)} %param.3) | copy-start | bytes 1572868
  18.7 1.5 %copy-start.4 = (f32[3,4,256,128]{3,2,1,0:T(8,128)S(1)}, f32[3,4,256,128]{3,2,1,0:T(8,128)}, u32[]{:S(2)}) copy-start(f32[3,4,256,128]{3,2,1,0:T(8,128)} %param.4) | copy-start | bytes 4718596
  21.4 1.0 %copy-start.2 = (f32[4,253,128]{2,1,0:T(8,128)S(1)}, f32[4,253,128]{2,1,0:T(8,128)}, u32[]{:S(2)}) copy-start(f32[4,253,128]{2,1,0:T(8,128)} %get-tuple-element.224) | copy-start | bytes 1554436
  21.4 1.2 %copy-start.3 = (f32[4,253,128]{2,1,0:T(8,128)S(1)}, f32[4,253,128]{2,1,0:T(8,128)}, u32[]{:S(2)}) copy-start(f32[4,253,128]{2,1,0:T(8,128)} %get-tuple-element.225) | copy-start | bytes 1554436
  23.2 1.0 %copy-start.1 = (f32[4,253,128]{2,1,0:T(8,128)S(1)}, f32[4,253,128]{2,1,0:T(8,128)}, u32[]{:S(2)}) copy-start(f32[4,253,128]{2,1,0:T(8,128)} %pad_slice_fusion.9) | copy-start | bytes 1554436
  33.2 19.1 %all-to-all-start = ((f32[16,4,8,128]{3,2,1,0:T(8,128)}), f32[16,4,8,128]{3,2,1,0:T(8,128)S(1)}, u32[]{:S(2)}, u32[]{:S(2)}) async-start(f32[16,4,8,128]{3,2,1,0:T(8,128)} %stack.2), calls=%async_computation | async-start | bytes 524288 | tf_op jit(solution)/shard_map/all_to_all | solution.py:111
